TPU v7x, 512 devices: a whole 4x4x16 slice. The times are simulated.
512 devices in a mesh: cand: 8 (over y, core), doc: 64 (over z, x).
Axes of the slice: x: 4, y: 4, z: 16, core: 2. Of those that a mesh axis runs over, the one named last changes fastest.
Arguments:
- queries: bfloat16 [8192, 8192], P('doc'), may hold values from -6 to 50
- keys_values: bfloat16 [2, 8192, 1024], P(None, 'doc', 'cand'), may hold values from -6 to 50
- factors: float32 [8, 64], P('cand'), may hold values from 1 to 16
- lengths: int32 [16], replicated, may hold values from 1 to 1024, 8192 in all
Outputs:
- attended: bfloat16 [8, 8192, 8192], P('cand', 'doc')
All inputs are finite; a program needn't handle non-finite values.
Results may differ from a plain program's by a relative error of at most 0.0053.
Values may be sent and summed in bfloat16 or wider, within the bound.
No kernel may reach another device: no remote copies, remote signals or barrier semaphores. Data moves between devices by JAX's collectives and lax.ppermute only.
A program may use at most 64 MiB of HBM per device.

v0:
```python
import math
import jax
import jax.numpy as jnp
from jax import lax
from jax.sharding import PartitionSpec as P

H = 64
KVH = 8
HD = 128
SPAN = 8
ROPE_BASE = 500000.0


def passed_along(value, axis, steps):
    count = lax.axis_size(axis)
    first, last = (max(0, -steps), min(count, count - steps))
    return lax.ppermute(value, axis, [(source, source + steps) for source in range(first, last)])


def locate(index_rows, lengths):
    ends = jnp.cumsum(lengths)
    starts = ends - lengths
    docid = jnp.sum((index_rows[:, None] >= ends[None, :]).astype(jnp.int32), axis=1)
    onehot = docid[:, None] == jnp.arange(lengths.shape[0], dtype=jnp.int32)[None, :]
    first_row = jnp.sum(jnp.where(onehot, starts[None, :], 0), axis=1)
    valid = index_rows >= 0
    return (jnp.where(valid, docid, -1), jnp.where(valid, index_rows - first_row, 0))


def rotate(values, offsets, factor):
    row_count = values.shape[0]
    heads_here = values.shape[1] // HD
    half_dim = HD // 2
    shaped = values.reshape(row_count, heads_here, HD).astype(jnp.float32)
    inverse = jnp.power(ROPE_BASE, -2.0 * jnp.arange(half_dim, dtype=jnp.float32) / HD) / factor
    angles = offsets.astype(jnp.float32)[:, None] * inverse[None, :]
    cosine = jnp.cos(angles)[:, None, :]
    sine = jnp.sin(angles)[:, None, :]
    first_half = shaped[..., :half_dim]
    second_half = shaped[..., half_dim:]
    turned = jnp.concatenate(
        [first_half * cosine - second_half * sine, second_half * cosine + first_half * sine],
        axis=-1,
    )
    return turned.reshape(row_count, heads_here * HD).astype(jnp.bfloat16)


def attend(query_rot, key_rot, value_rows, query_doc, query_index, key_doc, key_index):
    row_count = query_rot.shape[0]
    key_count = key_rot.shape[0]
    group_size = H // KVH
    q_grouped = query_rot.reshape(row_count, KVH, group_size, HD).transpose(1, 0, 2, 3)
    k_grouped = key_rot.reshape(key_count, KVH, HD).transpose(1, 0, 2)
    v_grouped = value_rows.reshape(key_count, KVH, HD).transpose(1, 0, 2)
    allowed = (
        (key_doc[None, :] == query_doc[:, None])
        & (key_index[None, :] <= query_index[:, None])
        & (key_doc[None, :] >= 0)
    )
    scale = 1.0 / math.sqrt(HD)

    def per_group(operands):
        q_part, k_part, v_part = operands
        scores = (
            jnp.einsum("rgd,wd->rgw", q_part, k_part, preferred_element_type=jnp.float32) * scale
        )
        scores = jnp.where(allowed[:, None, :], scores, -1e30)
        largest = jnp.max(scores, axis=-1, keepdims=True)
        expw = jnp.exp(scores - largest)
        total = jnp.sum(expw, axis=-1, keepdims=True)
        weights = expw.astype(jnp.bfloat16)
        numer = jnp.einsum("rgw,wd->rgd", weights, v_part, preferred_element_type=jnp.float32)
        return (numer / total).astype(jnp.bfloat16)

    mixed = lax.map(per_group, (q_grouped, k_grouped, v_grouped))
    return mixed.transpose(1, 0, 2, 3).reshape(row_count, H * HD)


def on_device(queries, keys_values, factors, lengths):
    row_count = queries.shape[0]
    device = lax.axis_index("doc")
    query_index = device * row_count + jnp.arange(row_count, dtype=jnp.int32)
    key_index = (device - SPAN) * row_count + jnp.arange((SPAN + 1) * row_count, dtype=jnp.int32)
    whole = lax.all_gather(keys_values, "cand", axis=2, tiled=True)
    pieces = []
    for distance in range(SPAN, 0, -1):
        pieces.append(passed_along(whole, "doc", distance))
    pieces.append(whole)
    window = jnp.concatenate(pieces, axis=1)
    query_doc, query_offset = locate(query_index, lengths)
    key_doc, key_offset = locate(key_index, lengths)
    factor = factors[0]
    query_rot = rotate(queries, query_offset, factor)
    key_rot = rotate(window[0], key_offset, factor)
    mixed = attend(query_rot, key_rot, window[1], query_doc, query_index, key_doc, key_index)
    return mixed[None]


def solution(mesh):
    placed = (P("doc", None), P(None, "doc", "cand"), P("cand", None), P())
    return jax.shard_map(
        on_device, mesh=mesh, in_specs=placed, out_specs=P("cand", "doc", None), check_vma=False
    )
```

profile of v0, /device:TPU:448, one launch (start us, length us, event | category | flops | bytes accessed | tf_op | source)
XLA Modules:
  0.0 222.4 jit_solution(7817300378528015322)
XLA Ops:
  1.0 13.6 %all_gather.3 = bf16[2,128,1024]{1,2,0:T(8,128)(2,1)S(1)} all-gather(bf16[2,128,128]{1,2,0:T(8,128)(2,1)S(1)} %copy.19), channel_id=1, replica_groups=mesh['cand'=8,'doc'=64] {'cand'}, dimensions={2}, use_global_device_ids=true | all-gather | bytes 589824 | tf_op jit(solution)/shard_map/all_gather | solution.py:84
  15.9 5.1 %collective-permute-start.1 = (bf16[2,128,1024]{1,2,0:T(8,128)(2,1)S(1)}, bf16[2,128,1024]{1,2,0:T(8,128)(2,1)S(1)}, u32[]{:S(2)}, u32[]{:S(2)}) collective-permute-start(bf16[2,128,1024]{1,2,0:T(8,128)(2,1)S(1)} %all_gather.3), channel_id=1, source_target_pairs={{0,7},{1,8},{2,9},{3,10},{4,11},{5,12},{6,13},{7,14},{8,15},{9,16}... | collective-permute-start | bytes 1572872 | tf_op jit(solution)/shard_map/ppermute | solution.py:17
  29.6 4.6 %fusion.35 = (f32[128,64,64]{2,1,0:T(8,128)}, f32[128,64,64]{2,1,0:T(8,128)}) fusion(f32[128,64,128]{2,1,0:T(8,128)S(1)} %bitcast.48), kind=kLoop, calls=%fused_computation.60 | loop fusion | bytes 8388608 | tf_op jit(solution)/shard_map/slice | solution.py:39
  35.1 8.3 %subtract_convert_fusion = (bf16[128,64,64]{2,0,1:T(8,128)(2,1)S(1)}, bf16[128,64,64]{2,0,1:T(8,128)(2,1)S(1)}) fusion(f32[128,64,64]{2,1,0:T(8,128)} %get-tuple-element.116, f32[128,64,64]{2,1,0:T(8,128)} %get-tuple-element.115, f32[128,64]{1,0:T(8,128)S(1)} %get-tuple-element.120, f32[128,64]{1,0:T(8,128)S(1)} %get-tuple-element.119), kind=kLoop, calls=%fused_computation.23 | loop fusion | flops 4194304 | bytes 6356992 | tf_op jit(solution)/shard_map/convert.4
  44.6 2.5 %pad_maximum_fusion = bf16[128,64,128]{2,0,1:T(8,128)(2,1)} fusion(bf16[128,64,64]{2,0,1:T(8,128)(2,1)S(1)} %get-tuple-element.110, bf16[128,64,64]{2,0,1:T(8,128)(2,1)S(1)} %get-tuple-element.109), kind=kLoop, calls=%fused_computation.27 | loop fusion | flops 4194304 | bytes 4194304 | tf_op jit(solution)/shard_map/concatenate | solution.py:41
  47.1 2.1 collective-permute-start.5
  50.3 16.4 %collective-permute-done.1 = bf16[2,128,1024]{1,2,0:T(8,128)(2,1)S(1)} collective-permute-done((bf16[2,128,1024]{1,2,0:T(8,128)(2,1)S(1)}, bf16[2,128,1024]{1,2,0:T(8,128)(2,1)S(1)}, u32[]{:S(2)}, u32[]{:S(2)}) %collective-permute-start.1) | collective-permute-done | bytes 524320 | tf_op jit(solution)/shard_map/ppermute | solution.py:17
  68.8 22.0 %collective-permute-done.2 = bf16[2,128,1024]{1,2,0:T(8,128)(2,1)S(1)} collective-permute-done((bf16[2,128,1024]{1,2,0:T(8,128)(2,1)S(1)}, bf16[2,128,1024]{1,2,0:T(8,128)(2,1)S(1)}, u32[]{:S(2)}, u32[]{:S(2)}) %collective-permute-start.2) | collective-permute-done | bytes 524320 | tf_op jit(solution)/shard_map/ppermute | solution.py:17
  92.9 20.1 %collective-permute-done.3 = bf16[2,128,1024]{1,2,0:T(8,128)(2,1)S(1)} collective-permute-done((bf16[2,128,1024]{1,2,0:T(8,128)(2,1)S(1)}, bf16[2,128,1024]{1,2,0:T(8,128)(2,1)S(1)}, u32[]{:S(2)}, u32[]{:S(2)}) %collective-permute-start.3) | collective-permute-done | bytes 524320 | tf_op jit(solution)/shard_map/ppermute | solution.py:17
  113.2 6.8 %collective-permute-done.5 = bf16[2,128,1024]{1,2,0:T(8,128)(2,1)S(1)} collective-permute-done((bf16[2,128,1024]{1,2,0:T(8,128)(2,1)S(1)}, bf16[2,128,1024]{1,2,0:T(8,128)(2,1)S(1)}, u32[]{:S(2)}, u32[]{:S(2)}) %collective-permute-start.5) | collective-permute-done | bytes 524320 | tf_op jit(solution)/shard_map/ppermute | solution.py:17
  120.1 14.6 %collective-permute-done.6 = bf16[2,128,1024]{1,2,0:T(8,128)(2,1)S(1)} collective-permute-done((bf16[2,128,1024]{1,2,0:T(8,128)(2,1)S(1)}, bf16[2,128,1024]{1,2,0:T(8,128)(2,1)S(1)}, u32[]{:S(2)}, u32[]{:S(2)}) %collective-permute-start.6) | collective-permute-done | bytes 524320 | tf_op jit(solution)/shard_map/ppermute | solution.py:17
  134.9 31.8 %collective-permute-done.7 = bf16[2,128,1024]{1,2,0:T(8,128)(2,1)S(1)} collective-permute-done((bf16[2,128,1024]{1,2,0:T(8,128)(2,1)S(1)}, bf16[2,128,1024]{1,2,0:T(8,128)(2,1)S(1)}, u32[]{:S(2)}, u32[]{:S(2)}) %collective-permute-start.7) | collective-permute-done | bytes 524320 | tf_op jit(solution)/shard_map/ppermute | solution.py:17
  169.9 47.3 %while.11 = (s32[]{:T(128)}, bf16[8,128,8,128]{3,1,2,0:T(8,128)(2,1)}, bf16[8,128,8,128]{3,1,2,0:T(8,128)(2,1)}, bf16[8,1152,128]{1,2,0:T(8,128)(2,1)S(1)}, bf16...) while((s32[]{:T(128)}, ...), condition=%wide.region_8.9_spmd.clone, body=%wide.region_5.8_spmd.clone.sunk | while | flops 613087232 | bytes 15598837 | solution.py:75
  173.2 2.6 %fusion.45 = bf16[8,128,8,128]{3,1,2,0:T(8,128)(2,1)} fusion(bf16[8,128,8,128]{3,1,2,0:T(8,128)(2,1)} %get-tuple-element.200, s32[]{:T(128)S(6)} %copy.43, f32[128,8,1152]{2,0,1:T(8,128)S(1)} %get-tuple-element.186, f32[128,8]{0,1:T(8,128)S(1)} %get-tuple-element.187, bf16[8,1152,128]{1,2,0:T(8,128)(2,1)} %get-tuple-element.214, ...), kind=kOutput, calls=%fused_computation.11.clone.1 | convolution fusion | flops 304611328 | bytes 5284864 | tf_op jit(solution)/shard_map/while/body/eval_jaxpr/rgw,wd->rgd/dot_general | solution.py:72
  179.1 2.6 %fusion.45 = bf16[8,128,8,128]{3,1,2,0:T(8,128)(2,1)} fusion(bf16[8,128,8,128]{3,1,2,0:T(8,128)(2,1)} %get-tuple-element.200, s32[]{:T(128)S(6)} %copy.43, f32[128,8,1152]{2,0,1:T(8,128)S(1)} %get-tuple-element.186, f32[128,8]{0,1:T(8,128)S(1)} %get-tuple-element.187, bf16[8,1152,128]{1,2,0:T(8,128)(2,1)} %get-tuple-element.214, ...), kind=kOutput, calls=%fused_computation.11.clone.1 | convolution fusion | flops 304611328 | bytes 5284864 | tf_op jit(solution)/shard_map/while/body/eval_jaxpr/rgw,wd->rgd/dot_general | solution.py:72
  182.0 2.1 fusion.43
  185.1 2.6 %fusion.45 = bf16[8,128,8,128]{3,1,2,0:T(8,128)(2,1)} fusion(bf16[8,128,8,128]{3,1,2,0:T(8,128)(2,1)} %get-tuple-element.200, s32[]{:T(128)S(6)} %copy.43, f32[128,8,1152]{2,0,1:T(8,128)S(1)} %get-tuple-element.186, f32[128,8]{0,1:T(8,128)S(1)} %get-tuple-element.187, bf16[8,1152,128]{1,2,0:T(8,128)(2,1)} %get-tuple-element.214, ...), kind=kOutput, calls=%fused_computation.11.clone.1 | convolution fusion | flops 304611328 | bytes 5284864 | tf_op jit(solution)/shard_map/while/body/eval_jaxpr/rgw,wd->rgd/dot_general | solution.py:72
  191.0 2.6 %fusion.45 = bf16[8,128,8,128]{3,1,2,0:T(8,128)(2,1)} fusion(bf16[8,128,8,128]{3,1,2,0:T(8,128)(2,1)} %get-tuple-element.200, s32[]{:T(128)S(6)} %copy.43, f32[128,8,1152]{2,0,1:T(8,128)S(1)} %get-tuple-element.186, f32[128,8]{0,1:T(8,128)S(1)} %get-tuple-element.187, bf16[8,1152,128]{1,2,0:T(8,128)(2,1)} %get-tuple-element.214, ...), kind=kOutput, calls=%fused_computation.11.clone.1 | convolution fusion | flops 304611328 | bytes 5284864 | tf_op jit(solution)/shard_map/while/body/eval_jaxpr/rgw,wd->rgd/dot_general | solution.py:72
  196.9 2.6 %fusion.45 = bf16[8,128,8,128]{3,1,2,0:T(8,128)(2,1)} fusion(bf16[8,128,8,128]{3,1,2,0:T(8,128)(2,1)} %get-tuple-element.200, s32[]{:T(128)S(6)} %copy.43, f32[128,8,1152]{2,0,1:T(8,128)S(1)} %get-tuple-element.186, f32[128,8]{0,1:T(8,128)S(1)} %get-tuple-element.187, bf16[8,1152,128]{1,2,0:T(8,128)(2,1)} %get-tuple-element.214, ...), kind=kOutput, calls=%fused_computation.11.clone.1 | convolution fusion | flops 304611328 | bytes 5284864 | tf_op jit(solution)/shard_map/while/body/eval_jaxpr/rgw,wd->rgd/dot_general | solution.py:72
  202.8 2.6 %fusion.45 = bf16[8,128,8,128]{3,1,2,0:T(8,128)(2,1)} fusion(bf16[8,128,8,128]{3,1,2,0:T(8,128)(2,1)} %get-tuple-element.200, s32[]{:T(128)S(6)} %copy.43, f32[128,8,1152]{2,0,1:T(8,128)S(1)} %get-tuple-element.186, f32[128,8]{0,1:T(8,128)S(1)} %get-tuple-element.187, bf16[8,1152,128]{1,2,0:T(8,128)(2,1)} %get-tuple-element.214, ...), kind=kOutput, calls=%fused_computation.11.clone.1 | convolution fusion | flops 304611328 | bytes 5284864 | tf_op jit(solution)/shard_map/while/body/eval_jaxpr/rgw,wd->rgd/dot_general | solution.py:72
  208.7 2.6 %fusion.45 = bf16[8,128,8,128]{3,1,2,0:T(8,128)(2,1)} fusion(bf16[8,128,8,128]{3,1,2,0:T(8,128)(2,1)} %get-tuple-element.200, s32[]{:T(128)S(6)} %copy.43, f32[128,8,1152]{2,0,1:T(8,128)S(1)} %get-tuple-element.186, f32[128,8]{0,1:T(8,128)S(1)} %get-tuple-element.187, bf16[8,1152,128]{1,2,0:T(8,128)(2,1)} %get-tuple-element.214, ...), kind=kOutput, calls=%fused_computation.11.clone.1 | convolution fusion | flops 304611328 | bytes 5284864 | tf_op jit(solution)/shard_map/while/body/eval_jaxpr/rgw,wd->rgd/dot_general | solution.py:72
  214.6 2.6 %fusion.45 = bf16[8,128,8,128]{3,1,2,0:T(8,128)(2,1)} fusion(bf16[8,128,8,128]{3,1,2,0:T(8,128)(2,1)} %get-tuple-element.200, s32[]{:T(128)S(6)} %copy.43, f32[128,8,1152]{2,0,1:T(8,128)S(1)} %get-tuple-element.186, f32[128,8]{0,1:T(8,128)S(1)} %get-tuple-element.187, bf16[8,1152,128]{1,2,0:T(8,128)(2,1)} %get-tuple-element.214, ...), kind=kOutput, calls=%fused_computation.11.clone.1 | convolution fusion | flops 304611328 | bytes 5284864 | tf_op jit(solution)/shard_map/while/body/eval_jaxpr/rgw,wd->rgd/dot_general | solution.py:72
  217.2 2.9 %copy.22 = bf16[128,8,8,128]{3,2,1,0:T(8,128)(2,1)S(1)} copy(bf16[128,8,8,128]{3,0,2,1:T(8,128)(2,1)} %bitcast.52) | data formatting | bytes 4194304 | tf_op jit(solution)/shard_map/transpose | solution.py:76
  220.1 2.3 %broadcast_in_dim_reshape.3 = bf16[1,128,8192]{2,1,0:T(8,128)(2,1)} reshape(bf16[128,8,8,128]{3,2,1,0:T(8,128)(2,1)S(1)} %copy.22) | data formatting | bytes 4194304 | tf_op jit(solution)/shard_map/broadcast_in_dim;reshape | solution.py:96
  (68 shorter events, 46.0 us)
Async XLA Ops:
  14.6 32.5 %collective-permute-start = (bf16[2,128,1024]{1,2,0:T(8,128)(2,1)S(1)}, bf16[2,128,1024]{1,2,0:T(8,128)(2,1)}, u32[]{:S(2)}, u32[]{:S(2)}) collective-permute-start(bf16[2,128,1024]{1,2,0:T(8,128)(2,1)S(1)} %all_gather.3), channel_id=1, source_target_pairs={{0,8},{1,9},{2,10},{3,11},{4,12},{5,13},{6,14},{7,15},{8,16},{9,17... | collective-permute-start | bytes 1572872 | tf_op jit(solution)/shard_map/ppermute | solution.py:17
  15.9 50.9 %collective-permute-start.1 = (bf16[2,128,1024]{1,2,0:T(8,128)(2,1)S(1)}, bf16[2,128,1024]{1,2,0:T(8,128)(2,1)S(1)}, u32[]{:S(2)}, u32[]{:S(2)}) collective-permute-start(bf16[2,128,1024]{1,2,0:T(8,128)(2,1)S(1)} %all_gather.3), channel_id=1, source_target_pairs={{0,7},{1,8},{2,9},{3,10},{4,11},{5,12},{6,13},{7,14},{8,15},{9,16}... | collective-permute-start | bytes 1572872 | tf_op jit(solution)/shard_map/ppermute | solution.py:17
  21.0 69.8 %collective-permute-start.2 = (bf16[2,128,1024]{1,2,0:T(8,128)(2,1)S(1)}, bf16[2,128,1024]{1,2,0:T(8,128)(2,1)S(1)}, u32[]{:S(2)}, u32[]{:S(2)}) collective-permute-start(bf16[2,128,1024]{1,2,0:T(8,128)(2,1)S(1)} %all_gather.3), channel_id=1, source_target_pairs={{0,6},{1,7},{2,8},{3,9},{4,10},{5,11},{6,12},{7,13},{8,14},{9,15},... | collective-permute-start | bytes 1572872 | tf_op jit(solution)/shard_map/ppermute | solution.py:17
  22.9 90.0 %collective-permute-start.3 = (bf16[2,128,1024]{1,2,0:T(8,128)(2,1)S(1)}, bf16[2,128,1024]{1,2,0:T(8,128)(2,1)S(1)}, u32[]{:S(2)}, u32[]{:S(2)}) collective-permute-start(bf16[2,128,1024]{1,2,0:T(8,128)(2,1)S(1)} %all_gather.3), channel_id=1, source_target_pairs={{0,5},{1,6},{2,7},{3,8},{4,9},{5,10},{6,11},{7,12},{8,13},{9,14},{... | collective-permute-start | bytes 1572872 | tf_op jit(solution)/shard_map/ppermute | solution.py:17
  24.9 88.2 %collective-permute-start.4 = (bf16[2,128,1024]{1,2,0:T(8,128)(2,1)S(1)}, bf16[2,128,1024]{1,2,0:T(8,128)(2,1)S(1)}, u32[]{:S(2)}, u32[]{:S(2)}) collective-permute-start(bf16[2,128,1024]{1,2,0:T(8,128)(2,1)S(1)} %all_gather.3), channel_id=1, source_target_pairs={{0,4},{1,5},{2,6},{3,7},{4,8},{5,9},{6,10},{7,11},{8,12},{9,13},{1... | collective-permute-start | bytes 1572872 | tf_op jit(solution)/shard_map/ppermute | solution.py:17
  29.5 4.6 %copy-start.1 = (f32[1,64]{1,0:T(1,128)S(1)}, f32[1,64]{1,0:T(1,128)}, u32[]{:S(2)}) copy-start(f32[1,64]{1,0:T(1,128)} %param.8) | copy-start | bytes 772
  29.6 4.6 %copy-start = (s32[16]{0:T(128)S(1)}, s32[16]{0:T(128)}, u32[]{:S(2)}) copy-start(s32[16]{0:T(128)} %param.9) | copy-start | bytes 196
  47.1 72.9 %collective-permute-start.5 = (bf16[2,128,1024]{1,2,0:T(8,128)(2,1)S(1)}, bf16[2,128,1024]{1,2,0:T(8,128)(2,1)S(1)}, u32[]{:S(2)}, u32[]{:S(2)}) collective-permute-start(bf16[2,128,1024]{1,2,0:T(8,128)(2,1)S(1)} %all_gather.3), channel_id=1, source_target_pairs={{0,3},{1,4},{2,5},{3,6},{4,7},{5,8},{6,9},{7,10},{8,11},{9,12},{10... | collective-permute-start | bytes 1572872 | tf_op jit(solution)/shard_map/ppermute | solution.py:17
  66.7 68.0 %collective-permute-start.6 = (bf16[2,128,1024]{1,2,0:T(8,128)(2,1)S(1)}, bf16[2,128,1024]{1,2,0:T(8,128)(2,1)S(1)}, u32[]{:S(2)}, u32[]{:S(2)}) collective-permute-start(bf16[2,128,1024]{1,2,0:T(8,128)(2,1)S(1)} %all_gather.3), channel_id=1, source_target_pairs={{0,2},{1,3},{2,4},{3,5},{4,6},{5,7},{6,8},{7,9},{8,10},{9,11},{10,... | collective-permute-start | bytes 1572872 | tf_op jit(solution)/shard_map/ppermute | solution.py:17
  90.8 75.9 %collective-permute-start.7 = (bf16[2,128,1024]{1,2,0:T(8,128)(2,1)S(1)}, bf16[2,128,1024]{1,2,0:T(8,128)(2,1)S(1)}, u32[]{:S(2)}, u32[]{:S(2)}) collective-permute-start(bf16[2,128,1024]{1,2,0:T(8,128)(2,1)S(1)} %all_gather.3), channel_id=1, source_target_pairs={{0,1},{1,2},{2,3},{3,4},{4,5},{5,6},{6,7},{7,8},{8,9},{9,10},{10,1... | collective-permute-start | bytes 1572872 | tf_op jit(solution)/shard_map/ppermute | solution.py:17
where the time goes:
time: 223 us; the launch traced here: 222 us
  waiting for transfers between devices  112 us (50%)
  matrix products  37.5 us (17%)
  other arithmetic  25.7 us (12%)
  starting transfers between devices  18.1 us (8%)
  local copies, waits for them, and re-layouts  15.5 us (7%)
  blocking collectives  13.6 us (6%)
    ppermute x8, waiting for transfers between devices, passed_along(): lax.ppermute(value, axis, [(source, source + steps) for source in range(f...  112 us
    dot_general x8, matrix products, per_group(): jnp.einsum('rgw,wd->rgd', weights, v_part, preferred_element_type=jnp.flo...  20.8 us
    ppermute x8, starting transfers between devices, passed_along(): lax.ppermute(value, axis, [(source, source + steps) for source in range(f...  18.1 us
    dot_general x8, matrix products, per_group(): jnp.einsum('rgd,wd->rgw', q_part, k_part, preferred_element_type=jnp.floa...  16.7 us
    all_gather x1, blocking collectives, on_device(): whole = lax.all_gather(keys_values, 'cand', axis=2, tiled=True)  13.6 us
    another operation x4, other arithmetic  9.14 us
    reduce_sum x8, other arithmetic, per_group(): total = jnp.sum(expw, axis=-1, keepdims=True)  8.08 us
    slice x1, local copies, waits for them, and re-layouts, rotate(): first_half = shaped[..., :half_dim]  4.58 us
  transfers between devices with their start and end apart: 8, of which 6 were waited for; matrix products, arithmetic and copies ran while one was open for 10% of the time, Pallas kernels for 0%

commit v1 on v0

--- a/solution.py
+++ b/solution.py
@@ -9,6 +9,12 @@
 HD = 128
 SPAN = 8
 ROPE_BASE = 500000.0
+
+
+def cover_group(my_tile):
+    o_now = jnp.stack(lax.axis_size("cand") * [my_tile])
+    view_out = lax.all_to_all(o_now, "cand", 0, 0)
+    return jnp.concatenate(view_out, axis=2)
 
 
 def passed_along(value, axis, steps):
@@ -81,7 +87,7 @@
     device = lax.axis_index("doc")
     query_index = device * row_count + jnp.arange(row_count, dtype=jnp.int32)
     key_index = (device - SPAN) * row_count + jnp.arange((SPAN + 1) * row_count, dtype=jnp.int32)
-    whole = lax.all_gather(keys_values, "cand", axis=2, tiled=True)
+    whole = cover_group(keys_values)
     pieces = []
     for distance in range(SPAN, 0, -1):
         pieces.append(passed_along(whole, "doc", distance))

time: 223 us -> 234 us (1.049)
  blocking collectives: 13.6 us -> 0 us
  waiting for transfers between devices: 112 us -> 120 us
  starting transfers between devices: 18.1 us -> 25.4 us
  local copies, waits for them, and re-layouts: 15.5 us -> 20.7 us
  other arithmetic: 25.7 us -> 28.5 us
    all_gather x1 -> x0, blocking collectives: 13.6 us -> none  [on_device(): whole = lax.all_gather(keys_values, 'cand', axis=2, tiled=True)]
    ppermute x8, waiting for transfers between devices: 112 us -> 120 us  [passed_along(): lax.ppermute(value, axis, [(source, source + steps) for source in range(f...]
    all_to_all x0 -> x1, starting transfers between devices: none -> 4.47 us  [cover_group(): view_out = lax.all_to_all(o_now, 'cand', 0, 0)]
    unnamed x14, local copies, waits for them, and re-layouts: 3.71 us -> 7.87 us
    ppermute x8, starting transfers between devices: 18.1 us -> 20.9 us  [passed_along(): lax.ppermute(value, axis, [(source, source + steps) for source in range(f...]
  transfers between devices with their start and end apart: 8 -> 9, of which waited for: 6 -> 7; matrix products, arithmetic and copies ran while one was open for 10% -> 13% of each run, Pallas kernels for 0% -> 0%
where the time goes in v1:
time: 234 us; the launch traced here: 233 us
  waiting for transfers between devices  120 us (51%)
  matrix products  37.5 us (16%)
  other arithmetic  28.5 us (12%)
  starting transfers between devices  25.4 us (11%)
  local copies, waits for them, and re-layouts  20.7 us (9%)
    ppermute x8, waiting for transfers between devices, passed_along(): lax.ppermute(value, axis, [(source, source + steps) for source in range(f...  120 us
    ppermute x8, starting transfers between devices, passed_along(): lax.ppermute(value, axis, [(source, source + steps) for source in range(f...  20.9 us
    dot_general x8, matrix products, per_group(): jnp.einsum('rgw,wd->rgd', weights, v_part, preferred_element_type=jnp.flo...  20.8 us
    dot_general x8, matrix products, per_group(): jnp.einsum('rgd,wd->rgw', q_part, k_part, preferred_element_type=jnp.floa...  16.7 us
    another operation x4, other arithmetic  10.5 us
    reduce_sum x8, other arithmetic, per_group(): total = jnp.sum(expw, axis=-1, keepdims=True)  8.08 us
    unnamed x14, local copies, waits for them, and re-layouts  7.87 us
  transfers between devices with their start and end apart: 9, of which 7 were waited for; matrix products, arithmetic and copies ran while one was open for 13% of the time, Pallas kernels for 0%

profile of v1, /device:TPU:448, one launch (start us, length us, event | category | flops | bytes accessed | tf_op | source)
XLA Modules:
  0.0 232.8 jit_solution(14266993190634364751)
XLA Ops:
  1.9 4.5 %all-to-all-start = ((bf16[8,2,128,128]{2,3,1,0:T(8,128)(2,1)}), bf16[8,2,128,128]{2,3,1,0:T(8,128)(2,1)S(1)}, u32[]{:S(2)}, u32[]{:S(2)}) async-start(bf16[8,2,128,128]{2,3,1,0:T(8,128)(2,1)} %stack.2), calls=%async_computation | async-start | bytes 1048576 | tf_op jit(solution)/shard_map/all_to_all | solution.py:16
  9.2 4.6 %fusion.35 = (f32[128,64,64]{2,1,0:T(8,128)}, f32[128,64,64]{2,1,0:T(8,128)}) fusion(f32[128,64,128]{2,1,0:T(8,128)S(1)} %bitcast.51), kind=kLoop, calls=%fused_computation.60 | loop fusion | bytes 8388608 | tf_op jit(solution)/shard_map/slice | solution.py:45
  14.7 9.7 %subtract_convert_fusion = (bf16[128,64,64]{2,0,1:T(8,128)(2,1)S(1)}, bf16[128,64,64]{2,0,1:T(8,128)(2,1)}) fusion(f32[128,64,64]{2,1,0:T(8,128)} %get-tuple-element.126, f32[128,64,64]{2,1,0:T(8,128)} %get-tuple-element.125, f32[128,64]{1,0:T(8,128)S(1)} %get-tuple-element.130, f32[128,64]{1,0:T(8,128)S(1)} %get-tuple-element.129), kind=kLoop, calls=%fused_computation.23 | loop fusion | flops 4194304 | bytes 6356992 | tf_op jit(solution)/shard_map/convert.4
  25.7 5.1 %collective-permute-start.1 = (bf16[2,128,1024]{1,2,0:T(8,128)(2,1)S(1)}, bf16[2,128,1024]{1,2,0:T(8,128)(2,1)}, u32[]{:S(2)}, u32[]{:S(2)}) collective-permute-start(bf16[2,128,1024]{1,2,0:T(8,128)(2,1)S(1)} %bitcast.57), channel_id=1, source_target_pairs={{0,7},{1,8},{2,9},{3,10},{4,11},{5,12},{6,13},{7,14},{8,15},{9,16}... | collective-permute-start | bytes 1572872 | tf_op jit(solution)/shard_map/ppermute | solution.py:23
  37.8 4.1 %pad_maximum_fusion = bf16[128,64,128]{2,0,1:T(8,128)(2,1)} fusion(bf16[128,64,64]{2,0,1:T(8,128)(2,1)} %get-tuple-element.120, bf16[128,64,64]{2,0,1:T(8,128)(2,1)S(1)} %get-tuple-element.119), kind=kLoop, calls=%fused_computation.27 | loop fusion | flops 4194304 | bytes 4194304 | tf_op jit(solution)/shard_map/concatenate | solution.py:47
  43.7 4.7 %collective-permute-start.5 = (bf16[2,128,1024]{1,2,0:T(8,128)(2,1)S(1)}, bf16[2,128,1024]{1,2,0:T(8,128)(2,1)S(1)}, u32[]{:S(2)}, u32[]{:S(2)}) collective-permute-start(bf16[2,128,1024]{1,2,0:T(8,128)(2,1)S(1)} %bitcast.61), channel_id=1, source_target_pairs={{0,3},{1,4},{2,5},{3,6},{4,7},{5,8},{6,9},{7,10},{8,11},{9,12},{10... | collective-permute-start | bytes 1572872 | tf_op jit(solution)/shard_map/ppermute | solution.py:23
  49.6 27.1 %collective-permute-done.1 = bf16[2,128,1024]{1,2,0:T(8,128)(2,1)} collective-permute-done((bf16[2,128,1024]{1,2,0:T(8,128)(2,1)S(1)}, bf16[2,128,1024]{1,2,0:T(8,128)(2,1)}, u32[]{:S(2)}, u32[]{:S(2)}) %collective-permute-start.1) | collective-permute-done | bytes 524320 | tf_op jit(solution)/shard_map/ppermute | solution.py:23
  79.8 20.9 %collective-permute-done.2 = bf16[2,128,1024]{1,2,0:T(8,128)(2,1)} collective-permute-done((bf16[2,128,1024]{1,2,0:T(8,128)(2,1)S(1)}, bf16[2,128,1024]{1,2,0:T(8,128)(2,1)}, u32[]{:S(2)}, u32[]{:S(2)}) %collective-permute-start.2) | collective-permute-done | bytes 524320 | tf_op jit(solution)/shard_map/ppermute | solution.py:23
  100.7 2.1 collective-permute-start.7
  104.0 18.9 %collective-permute-done.3 = bf16[2,128,1024]{1,2,0:T(8,128)(2,1)} collective-permute-done((bf16[2,128,1024]{1,2,0:T(8,128)(2,1)S(1)}, bf16[2,128,1024]{1,2,0:T(8,128)(2,1)}, u32[]{:S(2)}, u32[]{:S(2)}) %collective-permute-start.3) | collective-permute-done | bytes 524320 | tf_op jit(solution)/shard_map/ppermute | solution.py:23
  125.3 5.0 %collective-permute-done.5 = bf16[2,128,1024]{1,2,0:T(8,128)(2,1)S(1)} collective-permute-done((bf16[2,128,1024]{1,2,0:T(8,128)(2,1)S(1)}, bf16[2,128,1024]{1,2,0:T(8,128)(2,1)S(1)}, u32[]{:S(2)}, u32[]{:S(2)}) %collective-permute-start.5) | collective-permute-done | bytes 524320 | tf_op jit(solution)/shard_map/ppermute | solution.py:23
  130.4 14.4 %collective-permute-done.6 = bf16[2,128,1024]{1,2,0:T(8,128)(2,1)S(1)} collective-permute-done((bf16[2,128,1024]{1,2,0:T(8,128)(2,1)S(1)}, bf16[2,128,1024]{1,2,0:T(8,128)(2,1)S(1)}, u32[]{:S(2)}, u32[]{:S(2)}) %collective-permute-start.6) | collective-permute-done | bytes 524320 | tf_op jit(solution)/shard_map/ppermute | solution.py:23
  144.9 32.1 %collective-permute-done.7 = bf16[2,128,1024]{1,2,0:T(8,128)(2,1)S(1)} collective-permute-done((bf16[2,128,1024]{1,2,0:T(8,128)(2,1)S(1)}, bf16[2,128,1024]{1,2,0:T(8,128)(2,1)S(1)}, u32[]{:S(2)}, u32[]{:S(2)}) %collective-permute-start.7) | collective-permute-done | bytes 524320 | tf_op jit(solution)/shard_map/ppermute | solution.py:23
  180.2 47.3 %while.11 = (s32[]{:T(128)}, bf16[8,128,8,128]{3,1,2,0:T(8,128)(2,1)}, bf16[8,128,8,128]{3,1,2,0:T(8,128)(2,1)}, bf16[8,1152,128]{1,2,0:T(8,128)(2,1)S(1)}, bf16...) while((s32[]{:T(128)}, ...), condition=%wide.region_8.9_spmd.clone, body=%wide.region_5.8_spmd.clone.sunk | while | flops 613087232 | bytes 15598837 | solution.py:81
  183.6 2.6 %fusion.45 = bf16[8,128,8,128]{3,1,2,0:T(8,128)(2,1)} fusion(bf16[8,128,8,128]{3,1,2,0:T(8,128)(2,1)} %get-tuple-element.210, s32[]{:T(128)S(6)} %copy.52, f32[128,8,1152]{2,0,1:T(8,128)S(1)} %get-tuple-element.196, f32[128,8]{0,1:T(8,128)S(1)} %get-tuple-element.197, bf16[8,1152,128]{1,2,0:T(8,128)(2,1)} %get-tuple-element.224, ...), kind=kOutput, calls=%fused_computation.11.clone.1 | convolution fusion | flops 304611328 | bytes 5284864 | tf_op jit(solution)/shard_map/while/body/eval_jaxpr/rgw,wd->rgd/dot_general | solution.py:78
  189.5 2.6 %fusion.45 = bf16[8,128,8,128]{3,1,2,0:T(8,128)(2,1)} fusion(bf16[8,128,8,128]{3,1,2,0:T(8,128)(2,1)} %get-tuple-element.210, s32[]{:T(128)S(6)} %copy.52, f32[128,8,1152]{2,0,1:T(8,128)S(1)} %get-tuple-element.196, f32[128,8]{0,1:T(8,128)S(1)} %get-tuple-element.197, bf16[8,1152,128]{1,2,0:T(8,128)(2,1)} %get-tuple-element.224, ...), kind=kOutput, calls=%fused_computation.11.clone.1 | convolution fusion | flops 304611328 | bytes 5284864 | tf_op jit(solution)/shard_map/while/body/eval_jaxpr/rgw,wd->rgd/dot_general | solution.py:78
  195.4 2.6 %fusion.45 = bf16[8,128,8,128]{3,1,2,0:T(8,128)(2,1)} fusion(bf16[8,128,8,128]{3,1,2,0:T(8,128)(2,1)} %get-tuple-element.210, s32[]{:T(128)S(6)} %copy.52, f32[128,8,1152]{2,0,1:T(8,128)S(1)} %get-tuple-element.196, f32[128,8]{0,1:T(8,128)S(1)} %get-tuple-element.197, bf16[8,1152,128]{1,2,0:T(8,128)(2,1)} %get-tuple-element.224, ...), kind=kOutput, calls=%fused_computation.11.clone.1 | convolution fusion | flops 304611328 | bytes 5284864 | tf_op jit(solution)/shard_map/while/body/eval_jaxpr/rgw,wd->rgd/dot_general | solution.py:78
  201.3 2.6 %fusion.45 = bf16[8,128,8,128]{3,1,2,0:T(8,128)(2,1)} fusion(bf16[8,128,8,128]{3,1,2,0:T(8,128)(2,1)} %get-tuple-element.210, s32[]{:T(128)S(6)} %copy.52, f32[128,8,1152]{2,0,1:T(8,128)S(1)} %get-tuple-element.196, f32[128,8]{0,1:T(8,128)S(1)} %get-tuple-element.197, bf16[8,1152,128]{1,2,0:T(8,128)(2,1)} %get-tuple-element.224, ...), kind=kOutput, calls=%fused_computation.11.clone.1 | convolution fusion | flops 304611328 | bytes 5284864 | tf_op jit(solution)/shard_map/while/body/eval_jaxpr/rgw,wd->rgd/dot_general | solution.py:78
  207.2 2.6 %fusion.45 = bf16[8,128,8,128]{3,1,2,0:T(8,128)(2,1)} fusion(bf16[8,128,8,128]{3,1,2,0:T(8,128)(2,1)} %get-tuple-element.210, s32[]{:T(128)S(6)} %copy.52, f32[128,8,1152]{2,0,1:T(8,128)S(1)} %get-tuple-element.196, f32[128,8]{0,1:T(8,128)S(1)} %get-tuple-element.197, bf16[8,1152,128]{1,2,0:T(8,128)(2,1)} %get-tuple-element.224, ...), kind=kOutput, calls=%fused_computation.11.clone.1 | convolution fusion | flops 304611328 | bytes 5284864 | tf_op jit(solution)/shard_map/while/body/eval_jaxpr/rgw,wd->rgd/dot_general | solution.py:78
  213.1 2.6 %fusion.45 = bf16[8,128,8,128]{3,1,2,0:T(8,128)(2,1)} fusion(bf16[8,128,8,128]{3,1,2,0:T(8,128)(2,1)} %get-tuple-element.210, s32[]{:T(128)S(6)} %copy.52, f32[128,8,1152]{2,0,1:T(8,128)S(1)} %get-tuple-element.196, f32[128,8]{0,1:T(8,128)S(1)} %get-tuple-element.197, bf16[8,1152,128]{1,2,0:T(8,128)(2,1)} %get-tuple-element.224, ...), kind=kOutput, calls=%fused_computation.11.clone.1 | convolution fusion | flops 304611328 | bytes 5284864 | tf_op jit(solution)/shard_map/while/body/eval_jaxpr/rgw,wd->rgd/dot_general | solution.py:78
  219.0 2.6 %fusion.45 = bf16[8,128,8,128]{3,1,2,0:T(8,128)(2,1)} fusion(bf16[8,128,8,128]{3,1,2,0:T(8,128)(2,1)} %get-tuple-element.210, s32[]{:T(128)S(6)} %copy.52, f32[128,8,1152]{2,0,1:T(8,128)S(1)} %get-tuple-element.196, f32[128,8]{0,1:T(8,128)S(1)} %get-tuple-element.197, bf16[8,1152,128]{1,2,0:T(8,128)(2,1)} %get-tuple-element.224, ...), kind=kOutput, calls=%fused_computation.11.clone.1 | convolution fusion | flops 304611328 | bytes 5284864 | tf_op jit(solution)/shard_map/while/body/eval_jaxpr/rgw,wd->rgd/dot_general | solution.py:78
  224.9 2.6 %fusion.45 = bf16[8,128,8,128]{3,1,2,0:T(8,128)(2,1)} fusion(bf16[8,128,8,128]{3,1,2,0:T(8,128)(2,1)} %get-tuple-element.210, s32[]{:T(128)S(6)} %copy.52, f32[128,8,1152]{2,0,1:T(8,128)S(1)} %get-tuple-element.196, f32[128,8]{0,1:T(8,128)S(1)} %get-tuple-element.197, bf16[8,1152,128]{1,2,0:T(8,128)(2,1)} %get-tuple-element.224, ...), kind=kOutput, calls=%fused_computation.11.clone.1 | convolution fusion | flops 304611328 | bytes 5284864 | tf_op jit(solution)/shard_map/while/body/eval_jaxpr/rgw,wd->rgd/dot_general | solution.py:78
  227.5 2.9 %copy.31 = bf16[128,8,8,128]{3,2,1,0:T(8,128)(2,1)S(1)} copy(bf16[128,8,8,128]{3,0,2,1:T(8,128)(2,1)} %bitcast.55) | data formatting | bytes 4194304 | tf_op jit(solution)/shard_map/transpose | solution.py:82
  230.5 2.3 broadcast_in_dim_reshape.3
  (71 shorter events, 53.2 us)
Async XLA Ops:
  1.9 22.5 %all-to-all-start = ((bf16[8,2,128,128]{2,3,1,0:T(8,128)(2,1)}), bf16[8,2,128,128]{2,3,1,0:T(8,128)(2,1)S(1)}, u32[]{:S(2)}, u32[]{:S(2)}) async-start(bf16[8,2,128,128]{2,3,1,0:T(8,128)(2,1)} %stack.2), calls=%async_computation | async-start | bytes 1048576 | tf_op jit(solution)/shard_map/all_to_all | solution.py:16
  9.1 4.6 %copy-start.1 = (f32[1,64]{1,0:T(1,128)S(1)}, f32[1,64]{1,0:T(1,128)}, u32[]{:S(2)}) copy-start(f32[1,64]{1,0:T(1,128)} %param.8) | copy-start | bytes 772
  9.1 4.6 %copy-start = (s32[16]{0:T(128)S(1)}, s32[16]{0:T(128)}, u32[]{:S(2)}) copy-start(s32[16]{0:T(128)} %param.9) | copy-start | bytes 196
  24.4 19.3 %collective-permute-start = (bf16[2,128,1024]{1,2,0:T(8,128)(2,1)S(1)}, bf16[2,128,1024]{1,2,0:T(8,128)(2,1)}, u32[]{:S(2)}, u32[]{:S(2)}) collective-permute-start(bf16[2,128,1024]{1,2,0:T(8,128)(2,1)S(1)} %bitcast.56), channel_id=1, source_target_pairs={{0,8},{1,9},{2,10},{3,11},{4,12},{5,13},{6,14},{7,15},{8,16},{9,17... | collective-permute-start | bytes 1572872 | tf_op jit(solution)/shard_map/ppermute | solution.py:23
  25.7 51.0 %collective-permute-start.1 = (bf16[2,128,1024]{1,2,0:T(8,128)(2,1)S(1)}, bf16[2,128,1024]{1,2,0:T(8,128)(2,1)}, u32[]{:S(2)}, u32[]{:S(2)}) collective-permute-start(bf16[2,128,1024]{1,2,0:T(8,128)(2,1)S(1)} %bitcast.57), channel_id=1, source_target_pairs={{0,7},{1,8},{2,9},{3,10},{4,11},{5,12},{6,13},{7,14},{8,15},{9,16}... | collective-permute-start | bytes 1572872 | tf_op jit(solution)/shard_map/ppermute | solution.py:23
  32.0 68.8 %collective-permute-start.2 = (bf16[2,128,1024]{1,2,0:T(8,128)(2,1)S(1)}, bf16[2,128,1024]{1,2,0:T(8,128)(2,1)}, u32[]{:S(2)}, u32[]{:S(2)}) collective-permute-start(bf16[2,128,1024]{1,2,0:T(8,128)(2,1)S(1)} %bitcast.58), channel_id=1, source_target_pairs={{0,6},{1,7},{2,8},{3,9},{4,10},{5,11},{6,12},{7,13},{8,14},{9,15},... | collective-permute-start | bytes 1572872 | tf_op jit(solution)/shard_map/ppermute | solution.py:23
  33.9 89.0 %collective-permute-start.3 = (bf16[2,128,1024]{1,2,0:T(8,128)(2,1)S(1)}, bf16[2,128,1024]{1,2,0:T(8,128)(2,1)}, u32[]{:S(2)}, u32[]{:S(2)}) collective-permute-start(bf16[2,128,1024]{1,2,0:T(8,128)(2,1)S(1)} %bitcast.59), channel_id=1, source_target_pairs={{0,5},{1,6},{2,7},{3,8},{4,9},{5,10},{6,11},{7,12},{8,13},{9,14},{... | collective-permute-start | bytes 1572872 | tf_op jit(solution)/shard_map/ppermute | solution.py:23
  35.8 88.3 %collective-permute-start.4 = (bf16[2,128,1024]{1,2,0:T(8,128)(2,1)S(1)}, bf16[2,128,1024]{1,2,0:T(8,128)(2,1)}, u32[]{:S(2)}, u32[]{:S(2)}) collective-permute-start(bf16[2,128,1024]{1,2,0:T(8,128)(2,1)S(1)} %bitcast.60), channel_id=1, source_target_pairs={{0,4},{1,5},{2,6},{3,7},{4,8},{5,9},{6,10},{7,11},{8,12},{9,13},{1... | collective-permute-start | bytes 1572872 | tf_op jit(solution)/shard_map/ppermute | solution.py:23
  43.7 86.5 %collective-permute-start.5 = (bf16[2,128,1024]{1,2,0:T(8,128)(2,1)S(1)}, bf16[2,128,1024]{1,2,0:T(8,128)(2,1)S(1)}, u32[]{:S(2)}, u32[]{:S(2)}) collective-permute-start(bf16[2,128,1024]{1,2,0:T(8,128)(2,1)S(1)} %bitcast.61), channel_id=1, source_target_pairs={{0,3},{1,4},{2,5},{3,6},{4,7},{5,8},{6,9},{7,10},{8,11},{9,12},{10... | collective-permute-start | bytes 1572872 | tf_op jit(solution)/shard_map/ppermute | solution.py:23
  76.7 68.1 %collective-permute-start.6 = (bf16[2,128,1024]{1,2,0:T(8,128)(2,1)S(1)}, bf16[2,128,1024]{1,2,0:T(8,128)(2,1)S(1)}, u32[]{:S(2)}, u32[]{:S(2)}) collective-permute-start(bf16[2,128,1024]{1,2,0:T(8,128)(2,1)S(1)} %bitcast.62), channel_id=1, source_target_pairs={{0,2},{1,3},{2,4},{3,5},{4,6},{5,7},{6,8},{7,9},{8,10},{9,11},{10,... | collective-permute-start | bytes 1572872 | tf_op jit(solution)/shard_map/ppermute | solution.py:23
  100.7 76.3 %collective-permute-start.7 = (bf16[2,128,1024]{1,2,0:T(8,128)(2,1)S(1)}, bf16[2,128,1024]{1,2,0:T(8,128)(2,1)S(1)}, u32[]{:S(2)}, u32[]{:S(2)}) collective-permute-start(bf16[2,128,1024]{1,2,0:T(8,128)(2,1)S(1)} %bitcast.63), channel_id=1, source_target_pairs={{0,1},{1,2},{2,3},{3,4},{4,5},{5,6},{6,7},{7,8},{8,9},{9,10},{10,1... | collective-permute-start | bytes 1572872 | tf_op jit(solution)/shard_map/ppermute | solution.py:23
